TPU v7x, 256 devices: a whole 4x4x8 slice. The times are simulated.
256 devices in a mesh: ctx: 32 (over z, x), kvh: 8 (over y, core).
Axes of the slice: x: 4, y: 4, z: 8, core: 2. Of those that a mesh axis runs over, the one named last changes fastest.
Arguments:
- queries: bfloat16 [12288, 8192], P(('ctx', 'kvh')), may hold values from -150 to 150
- keys: bfloat16 [12288, 1024], P(('ctx', 'kvh')), may hold values from -6 to 6
- values: bfloat16 [12288, 1024], P(('ctx', 'kvh')), may hold values from -6 to 6
- doc_ids: int32 [12288], P('ctx'), may hold values from 0 to 7, never falling along the last dimension, each value on 1 to 6528 neighbouring positions
- block_keep: int32 [96, 96], P('ctx'), may hold values 0 or 1
Outputs:
- attended: bfloat16 [12288, 8192], P(('ctx', 'kvh'))
Inputs may be any that keep to these rules, and one draw needn't show every extreme that they name: `doc_ids`: never falls along the sequence; every document holds 1 to 6528 tokens and one holds exactly 6528.
All inputs are finite; a program needn't handle non-finite values. No bound on the sum of `block_keep` on one device may be relied on, other than what follows from the above.
Results may differ from a plain program's by a relative error of at most 0.004.
Values may be sent and summed in bfloat16 or wider, within the bound.
No kernel may reach another device: no remote copies, remote signals or barrier semaphores. Data moves between devices by JAX's collectives and lax.ppermute only.
A program may use at most 64 MiB of HBM per device.

v0:
```python
import functools

import numpy as np

import jax
import jax.numpy as jnp
from jax import lax
from jax.experimental import pallas as pl
from jax.experimental.pallas import tpu as pltpu
from jax.sharding import PartitionSpec as P

HD = 128
BLOCK = 128
NX = 4
N_DOC_IDS = 8
KEY_GROUP = 4


def attn_kernel(
    tab_ref, cnt_ref, keep_ref, base_ref,
    qds_ref, q_ref, kv_ref, *rest,
    heads, window, first, last, row_base,
):
    if first:
        state_in = ()
    else:
        state_in, rest = rest[:3], rest[3:]
    outs, (m_sc, l_sc, acc_sc) = rest[:-3], rest[-3:]
    qbl = pl.program_id(0)
    qpos0 = base_ref[0] + qbl * BLOCK
    scale = HD ** (-0.5)
    width = heads * BLOCK
    qpos = qpos0 + lax.broadcasted_iota(jnp.int32, (BLOCK, BLOCK), 1)
    krel = lax.broadcasted_iota(jnp.int32, (BLOCK, BLOCK), 0)
    qds = qds_ref[pl.ds(qbl, 1), :]
    qmat = q_ref[...].reshape(width, HD)

    if first:
        m_sc[...] = jnp.full(m_sc.shape, -1e30, jnp.float32)
        l_sc[...] = jnp.zeros(l_sc.shape, jnp.float32)
        acc_sc[...] = jnp.zeros(acc_sc.shape, jnp.float32)
    else:
        acc_in, m_in, l_in = state_in
        acc_sc[...] = acc_in[...]
        m_sc[...] = m_in[0:1, :]
        l_sc[...] = l_in[0:1, :]

    def mask_of(kb):
        kpos = kb * BLOCK + krel
        keep = keep_ref[qbl, kb]
        earlier = (kpos < qpos) & (qpos - kpos < window) & (kpos >= qds) & (keep != 0)
        return (kpos == qpos) | earlier

    def absorb(ents, masked):
        starts = [pl.multiple_of((rb - row_base) * 16, 16) for _, rb, _, _ in ents]
        k = jnp.concatenate([kv_ref[pl.ds(st, BLOCK), :HD] for st in starts], axis=0)
        v = jnp.concatenate([kv_ref[pl.ds(st, BLOCK), HD:] for st in starts], axis=0)
        s = lax.dot_general(
            k, qmat, (((1,), (1,)), ((), ())), preferred_element_type=jnp.float32
        ) * scale
        if masked:
            allowed = jnp.concatenate(
                [
                    (mask_of(kb) | (kind == 0)) & valid
                    for kb, _, kind, valid in ents
                ],
                axis=0,
            )
            s = jnp.where(jnp.tile(allowed, (1, heads)), s, -1e30)
        m_prev = m_sc[...]
        m_new = jnp.maximum(m_prev, jnp.max(s, axis=0, keepdims=True))
        alpha = jnp.exp(m_prev - m_new)
        p = jnp.exp(s - m_new)
        l_sc[...] = alpha * l_sc[...] + jnp.sum(p, axis=0, keepdims=True)
        acc_sc[...] = acc_sc[...] * alpha + lax.dot_general(
            v, p.astype(jnp.bfloat16), (((0,), (0,)), ((), ())),
            preferred_element_type=jnp.float32,
        )
        m_sc[...] = m_new

    lo = cnt_ref[qbl, 0]
    hi = cnt_ref[qbl, 1]

    def body(i, carry):
        n = lo + KEY_GROUP * i
        ents = []
        any_masked = False
        for j in range(KEY_GROUP):
            e = tab_ref[qbl, jnp.minimum(n + j, hi - 1)]
            valid = n + j < hi
            kind = jnp.where(valid, e >> 20, 1)
            ents.append((e & 255, (e >> 8) & 4095, kind, valid))
            any_masked = any_masked | (kind != 0)

        @pl.when(jnp.logical_not(any_masked))
        def _():
            absorb(ents, False)

        @pl.when(any_masked)
        def _():
            absorb(ents, True)

        return carry

    lax.fori_loop(0, (hi - lo + KEY_GROUP - 1) // KEY_GROUP, body, 0)

    if last:
        (o_ref,) = outs
        out = acc_sc[...] / l_sc[...]
        for h in range(heads):
            o_ref[:, h * HD:(h + 1) * HD] = out[:, h * BLOCK:(h + 1) * BLOCK].T.astype(o_ref.dtype)
    else:
        acc_o, m_o, l_o = outs
        acc_o[...] = acc_sc[...]
        m_o[...] = jnp.broadcast_to(m_sc[...], m_o.shape)
        l_o[...] = jnp.broadcast_to(l_sc[...], l_o.shape)


def block_tables(doc_start_q, keep_rows, first_blk, nkb, window, slot_of, own_rows):
    nqb = keep_rows.shape[0]
    nwin = window // BLOCK
    ds_blocks = doc_start_q.reshape(nqb, BLOCK)
    ds_first = ds_blocks[:, :1]
    ds_last = ds_blocks[:, -1:]
    qb = first_blk + jnp.arange(nqb, dtype=jnp.int32)[:, None]
    kb = jnp.arange(nkb, dtype=jnp.int32)[None, :]
    diag = kb == qb
    inwin = (kb <= qb) & (kb >= qb - nwin)
    keep = keep_rows == 1
    needed = inwin & (diag | (keep & (kb * BLOCK + BLOCK - 1 >= ds_first)))
    full = needed & (~diag) & (kb > qb - nwin) & (kb * BLOCK >= ds_last) & keep
    row_blk = jnp.clip(slot_of(kb), 0, 4095)
    own = row_blk < own_rows
    rank = jnp.where(diag, 0, jnp.where(full, 1, 2))
    sort_key = jnp.where(needed, jnp.where(own, rank, 3 + rank), 6).astype(jnp.int32)
    payload = (kb + 256 * row_blk + (1 << 20) * jnp.where(full, 0, 1)).astype(jnp.int32)
    payload = jnp.broadcast_to(payload, sort_key.shape)
    _, tab = lax.sort((sort_key, payload), dimension=1, is_stable=True, num_keys=1)
    n_own = jnp.sum(needed & own, axis=1).astype(jnp.int32)
    n_all = jnp.sum(needed, axis=1).astype(jnp.int32)
    zero = jnp.zeros_like(n_own)
    return tab, jnp.stack([zero, n_own], 1), jnp.stack([n_own, n_all], 1), ds_blocks


def attend_call(tab, cnt, keep_rows, base, ds_blocks, q_t, kv, state, *, window, first, last, row_base):
    heads, rows_here, _ = q_t.shape
    nqb = rows_here // BLOCK
    width = heads * BLOCK
    nk = kv.shape[0]
    kernel = functools.partial(
        attn_kernel, heads=heads, window=window, first=first, last=last, row_base=row_base
    )
    in_specs = [
        pl.BlockSpec((nqb, BLOCK), lambda i, *_: (0, 0)),
        pl.BlockSpec((heads, BLOCK, HD), lambda i, *_: (0, i, 0)),
        pl.BlockSpec((nk, 2 * HD), lambda i, *_: (0, 0)),
    ]
    state_specs = [
        pl.BlockSpec((HD, width), lambda i, *_: (i, 0)),
        pl.BlockSpec((8, width), lambda i, *_: (i, 0)),
        pl.BlockSpec((8, width), lambda i, *_: (i, 0)),
    ]
    state_shapes = [
        jax.ShapeDtypeStruct((nqb * HD, width), jnp.float32),
        jax.ShapeDtypeStruct((nqb * 8, width), jnp.float32),
        jax.ShapeDtypeStruct((nqb * 8, width), jnp.float32),
    ]
    args = [tab, cnt, keep_rows, base, ds_blocks, q_t, kv]
    if not first:
        in_specs += state_specs
        args += list(state)
    if last:
        out_specs = pl.BlockSpec((BLOCK, width), lambda i, *_: (i, 0))
        out_shape = jax.ShapeDtypeStruct((rows_here, width), q_t.dtype)
    else:
        out_specs = state_specs
        out_shape = state_shapes
    grid_spec = pltpu.PrefetchScalarGridSpec(
        num_scalar_prefetch=4,
        grid=(nqb,),
        in_specs=in_specs,
        out_specs=out_specs,
        scratch_shapes=[
            pltpu.VMEM((1, width), jnp.float32),
            pltpu.VMEM((1, width), jnp.float32),
            pltpu.VMEM((HD, width), jnp.float32),
        ],
    )
    flops = 4 * rows_here * heads * HD * BLOCK * 8
    cost = pl.CostEstimate(flops=flops, transcendentals=flops // (4 * HD), bytes_accessed=nk * 4 * HD)
    return pl.pallas_call(
        kernel, grid_spec=grid_spec, out_shape=out_shape, cost_estimate=cost
    )(*args)


def attention(q_local, kv_own, kv_rest, doc_start_q, keep_rows, first_row, window, nkb, slot_of):
    rows_here = q_local.shape[0]
    heads = q_local.shape[1] // HD
    first_blk = first_row // BLOCK
    own_rows = kv_own.shape[0] // 16
    tab, cnt_a, cnt_b, ds_blocks = block_tables(
        doc_start_q, keep_rows, first_blk, nkb, window, slot_of, own_rows
    )
    base = jnp.reshape(first_row, (1,)).astype(jnp.int32)
    keep_i = keep_rows.astype(jnp.int32)
    q_t = jnp.transpose(q_local.reshape(rows_here, heads, HD), (1, 0, 2))
    state = attend_call(
        tab, cnt_a, keep_i, base, ds_blocks, q_t, kv_own, None,
        window=window, first=True, last=False, row_base=0,
    )
    return attend_call(
        tab, cnt_b, keep_i, base, ds_blocks, q_t, kv_rest, state,
        window=window, first=False, last=True, row_base=own_rows,
    )


def shift(x, pairs):
    return lax.ppermute(x, "ctx", pairs)


def local(queries, keys, values, doc_ids, block_keep):
    rows_in = keys.shape[0]
    groups = keys.shape[1] // HD
    kv = jnp.concatenate(
        [keys.reshape(rows_in, groups, HD), values.reshape(rows_in, groups, HD)], axis=2
    ).reshape(rows_in, -1)
    kv_local = lax.all_to_all(kv, "kvh", split_axis=1, concat_axis=0, tiled=True)
    query_local = lax.all_to_all(queries, "kvh", split_axis=1, concat_axis=0, tiled=True)
    rows_here = query_local.shape[0]
    per_dev = rows_here // BLOCK
    n_ctx = lax.axis_size("ctx")
    nx = NX
    nz = n_ctx // nx
    reach = n_ctx // 2 // nx
    window = (n_ctx // 2) * rows_here
    ctx = lax.axis_index("ctx")
    first_row = ctx * rows_here
    zq, xq = ctx // nx, ctx % nx

    def x_pairs(d):
        return [(z * nx + x, z * nx + (x + d) % nx) for z in range(nz) for x in range(nx)]

    docs = jnp.arange(N_DOC_IDS, dtype=jnp.int32)
    below = jnp.sum((doc_ids[None, :] < docs[:, None]).astype(jnp.int32), axis=1)
    below_x = jnp.stack(
        [below] + [shift(below, x_pairs(d)) for d in range(1, nx)], axis=0
    ).reshape(-1)
    tail = jnp.zeros((16, kv_local.shape[1]), jnp.float32)
    tail = tail.at[0, :nx * N_DOC_IDS].set((below_x // 32).astype(jnp.float32))
    tail = tail.at[1, :nx * N_DOC_IDS].set((below_x % 32).astype(jnp.float32))
    piece = jnp.concatenate([kv_local, tail.astype(kv_local.dtype)], axis=0)
    prow = piece.shape[0]

    z_step = [(c, (c + nx) % n_ctx) for c in range(n_ctx)]

    col = [piece]
    for _ in range(reach):
        col.append(shift(col[-1], z_step))
    half = (reach + 1) // 2
    early = list(range(1, half + 1))
    late = list(range(half + 1, reach))
    parts, tags = list(col), [(a, 0) for a in range(reach + 1)]

    def add(arr, tag_list):
        parts.append(arr)
        tags.extend(tag_list)

    def blocks(idx):
        return jnp.concatenate([col[a] for a in idx], axis=0) if len(idx) > 1 else col[idx[0]]

    e_plus = shift(blocks(early), x_pairs(1))
    e_minus = shift(blocks(early), x_pairs(nx - 1))
    add(e_plus, [(a, 1) for a in early])
    add(e_minus, [(a, nx - 1) for a in early])
    add(shift(e_plus, x_pairs(1)), [(a, 2) for a in early])
    extra = {d: jnp.where(xq + d < nx, col[0], col[reach]) for d in range(1, nx)}
    l_plus = shift(jnp.concatenate([col[a] for a in late] + [extra[1]], axis=0), x_pairs(1))
    l_minus = shift(jnp.concatenate([col[a] for a in late] + [extra[nx - 1]], axis=0), x_pairs(nx - 1))
    add(l_plus, [(a, 1) for a in late] + [("e", 1)])
    add(l_minus, [(a, nx - 1) for a in late] + [("e", nx - 1)])
    if late:
        relay = l_minus[: prow * len(late)]
        add(shift(relay, x_pairs(nx - 1)), [(a, 2) for a in late])
    add(shift(extra[2], x_pairs(2)), [("e", 2)])
    kv_own = jnp.concatenate(parts[:reach + 1], axis=0)
    kv_rest = jnp.concatenate(parts[reach + 1:], axis=0)

    n_slots = len(tags)
    table = np.zeros((reach + 1, nx), np.int32)
    for s, (a, d) in enumerate(tags):
        if a == "e":
            table[0, d] = s
            table[reach, d] = s
        else:
            table[a, d] = s
    tails = kv_own.reshape(reach + 1, prow, -1)[:, rows_here:rows_here + 2, :nx * N_DOC_IDS]
    tails = tails.astype(jnp.int32)
    below_col = (tails[:, 0, :] * 32 + tails[:, 1, :]).reshape(reach + 1, nx, N_DOC_IDS)
    a_ids = np.arange(reach + 1)[:, None]
    d_ids = np.arange(nx)[None, :]
    src_ctx = (zq - a_ids) * nx + (xq - d_ids) % nx
    floor_ctx = jnp.maximum(ctx - reach * nx, 0)
    use = (src_ctx >= floor_ctx) & (src_ctx <= ctx)
    below_sum = jnp.sum(jnp.where(use[:, :, None], below_col, 0), axis=(0, 1))
    onehot = doc_ids[:, None] == docs[None, :]
    doc_start = floor_ctx * rows_here + jnp.sum(jnp.where(onehot, below_sum[None, :], 0), axis=1)

    def slot_of(kb):
        cp = kb // per_dev
        a = zq - cp // nx
        d = (xq - cp % nx) % nx
        hit = (a[..., None, None] == np.arange(reach + 1)[:, None]) & (
            d[..., None, None] == np.arange(nx)[None, :]
        )
        slot = jnp.sum(jnp.where(hit, table, 0), axis=(-2, -1))
        return (slot * prow + (kb % per_dev) * BLOCK) // 16

    outputs = attention(
        query_local, kv_own, kv_rest, doc_start.astype(jnp.int32), block_keep, first_row,
        window, n_ctx * per_dev, slot_of,
    )
    return lax.all_to_all(outputs, "kvh", split_axis=0, concat_axis=1, tiled=True)


def solution(mesh):
    return jax.shard_map(
        local,
        mesh=mesh,
        in_specs=(
            P(("ctx", "kvh"), None),
            P(("ctx", "kvh"), None),
            P(("ctx", "kvh"), None),
            P("ctx"),
            P("ctx", None),
        ),
        out_specs=P(("ctx", "kvh"), None),
        check_vma=False,
    )
```

profile of v0, /device:TPU:166, one launch (start us, length us, event | category | flops | bytes accessed | tf_op | source)
XLA Modules:
  0.0 124.3 jit_solution(6875314148552093608)
XLA Ops:
  0.0 0.8 convert_reduce_fusion.2
  0.8 0.9 collective-permute-start.2
  1.7 1.1 collective-permute-start.1
  2.8 2.1 %collective-permute-start = (s32[8]{0:T(128)S(1)}, s32[8]{0:T(128)S(1)}, u32[]{:S(2)}, u32[]{:S(2)}) collective-permute-start(s32[8]{0:T(128)S(1)} %convert_reduce_fusion.2), channel_id=1, source_target_pairs={{0,8},{8,16},{16,24},{24,0},{32,40},{40,48},{48,56},{56,32},{64,72... | collective-permute-start | bytes 104 | tf_op jit(solution)/shard_map/ppermute | solution.py:218
  4.9 0.9 copy_bitcast_fusion.2
  6.6 4.5 %all-to-all-start = ((bf16[48,8,256]{2,0,1:T(8,128)(2,1)}), bf16[48,8,256]{2,0,1:T(8,128)(2,1)S(1)}, u32[]{:S(2)}, u32[]{:S(2)}) async-start(bf16[48,8,256]{2,0,1:T(8,128)(2,1)} %pad_maximum_fusion.3), calls=%async_computation | async-start | bytes 393216 | tf_op jit(solution)/shard_map/all_to_all | solution.py:227
  13.3 2.1 %copy.52 = bf16[6,8,8,1024]{3,2,0,1:T(8,128)(2,1)} copy(bf16[6,8,8,1024]{3,2,1,0:T(8,128)(2,1)} %bitcast.48) | data formatting | bytes 1572864 | tf_op jit(solution)/shard_map/all_to_all | solution.py:228
  15.7 2.1 %all-to-all-done = bf16[48,8,256]{2,0,1:T(8,128)(2,1)S(1)} async-done(((bf16[48,8,256]{2,0,1:T(8,128)(2,1)}), bf16[48,8,256]{2,0,1:T(8,128)(2,1)S(1)}, u32[]{:S(2)}, u32[]{:S(2)}) %all-to-all-start) | async-done | bytes 196640 | tf_op jit(solution)/shard_map/all_to_all | solution.py:227
  17.9 3.5 %all-to-all-start.1 = ((bf16[48,8,1024]{2,0,1:T(8,128)(2,1)}), bf16[48,8,1024]{2,0,1:T(8,128)(2,1)S(1)}, u32[]{:S(2)}, u32[]{:S(2)}) async-start(bf16[48,8,1024]{2,0,1:T(8,128)(2,1)} %bitcast.40), calls=%async_computation.1 | async-start | bytes 1572864 | tf_op jit(solution)/shard_map/all_to_all | solution.py:228
  21.5 1.1 collective-permute-start.3
  22.9 6.1 %collective-permute-done.3 = bf16[400,256]{1,0:T(8,128)(2,1)S(1)} collective-permute-done((bf16[400,256]{1,0:T(8,128)(2,1)S(1)}, bf16[400,256]{1,0:T(8,128)(2,1)S(1)}, u32[]{:S(2)}, u32[]{:S(2)}) %collective-permute-start.3) | collective-permute-done | bytes 204832 | tf_op jit(solution)/shard_map/ppermute | solution.py:218
  28.9 1.0 collective-permute-start.4
  30.7 5.4 %collective-permute-done.4 = bf16[400,256]{1,0:T(8,128)(2,1)S(1)} collective-permute-done((bf16[400,256]{1,0:T(8,128)(2,1)S(1)}, bf16[400,256]{1,0:T(8,128)(2,1)S(1)}, u32[]{:S(2)}, u32[]{:S(2)}) %collective-permute-start.4) | collective-permute-done | bytes 204832 | tf_op jit(solution)/shard_map/ppermute | solution.py:218
  37.2 0.8 constant_dynamic-update-slice_fusion.7
  38.0 5.0 %collective-permute-done.5 = bf16[400,256]{1,0:T(8,128)(2,1)S(1)} collective-permute-done((bf16[400,256]{1,0:T(8,128)(2,1)S(1)}, bf16[400,256]{1,0:T(8,128)(2,1)S(1)}, u32[]{:S(2)}, u32[]{:S(2)}) %collective-permute-start.5) | collective-permute-done | bytes 204832 | tf_op jit(solution)/shard_map/ppermute | solution.py:218
  43.0 0.8 constant_dynamic-update-slice_fusion.6
  43.8 0.9 collective-permute-start.7
  44.7 1.1 collective-permute-start.8
  46.0 1.0 copy.53
  47.7 2.0 %collective-permute-done.6 = bf16[400,256]{1,0:T(8,128)(2,1)S(1)} collective-permute-done((bf16[400,256]{1,0:T(8,128)(2,1)S(1)}, bf16[400,256]{1,0:T(8,128)(2,1)S(1)}, u32[]{:S(2)}, u32[]{:S(2)}) %collective-permute-start.6) | collective-permute-done | bytes 204832 | tf_op jit(solution)/shard_map/ppermute | solution.py:218
  49.7 0.8 broadcast_select_fusion
  51.9 1.7 %sort.23 = (s32[3,96]{0,1:T(8,128)}, s32[3,96]{0,1:T(8,128)S(1)}, s32[3,96]{0,1:T(8,128)}) sort(s32[3,96]{0,1:T(8,128)S(1)} %get-tuple-element.58, s32[3,96]{0,1:T(8,128)S(1)} %get-tuple-element.57, s32[3,96]{0,1:T(8,128)S(1)} %iota.44), dimensions={1}, to_apply=%region_5.6 | sort | flops 2592 | bytes 6912 | tf_op jit(solution)/shard_map/sort | solution.py:138
  54.3 1.0 collective-permute-start.10
  55.3 1.1 collective-permute-start.11
  56.4 2.1 %collective-permute-start.13 = (bf16[400,256]{1,0:T(8,128)(2,1)S(1)}, bf16[400,256]{1,0:T(8,128)(2,1)S(1)}, u32[]{:S(2)}, u32[]{:S(2)}) collective-permute-start(bf16[400,256]{1,0:T(8,128)(2,1)S(1)} %get-tuple-element.47), channel_id=1, source_target_pairs={{0,16},{8,24},{16,0},{24,8},{32,48},{40,56},{48,32},{56,40},{64,80... | collective-permute-start | bytes 614408 | tf_op jit(solution)/shard_map/ppermute | solution.py:218
  61.6 12.3 %shard_map.100 = (f32[384,1024]{1,0:T(8,128)}, f32[24,1024]{1,0:T(8,128)}, f32[24,1024]{1,0:T(8,128)}) custom-call(s32[3,96]{1,0:T(4,128)} %copy.39.tab_ref, s32[3,2]{1,0:T(4,128)} %get-tuple-element.59.cnt_ref, s32[3,96]{1,0:T(4,128)} %keep_ref.3, s32[1]{0:T(128)} %bitcast.13.base_ref, s32[3,128]{1,0:T(4,128)} %copy-done.1, bf16[8,384,128]{2,1,0:T(8,128)(2,1)} %bitcast.49, ...), custom_call_target="tpu_custom_call" | custom-call | flops 1610612736 | bytes 1024000 | tf_op jit(solution)/shard_map/pallas_call | solution.py:191
  74.0 1.6 %collective-permute-done.9 = bf16[800,256]{1,0:T(8,128)(2,1)S(1)} collective-permute-done((bf16[800,256]{1,0:T(8,128)(2,1)S(1)}, bf16[800,256]{1,0:T(8,128)(2,1)S(1)}, u32[]{:S(2)}, u32[]{:S(2)}) %collective-permute-start.9) | collective-permute-done | bytes 409632 | tf_op jit(solution)/shard_map/ppermute | solution.py:218
  76.4 0.8 constant_dynamic-update-slice_fusion.11
  78.0 3.0 %collective-permute-done.12 = bf16[400,256]{1,0:T(8,128)(2,1)S(1)} collective-permute-done((bf16[400,256]{1,0:T(8,128)(2,1)S(1)}, bf16[400,256]{1,0:T(8,128)(2,1)S(1)}, u32[]{:S(2)}, u32[]{:S(2)}) %collective-permute-start.12) | collective-permute-done | bytes 204832 | tf_op jit(solution)/shard_map/ppermute | solution.py:218
  82.4 23.6 %shard_map.101 = bf16[384,1024]{1,0:T(8,128)(2,1)} custom-call(s32[3,96]{1,0:T(4,128)} %copy.39.tab_ref, s32[3,2]{1,0:T(4,128)} %get-tuple-element.60.cnt_ref, s32[3,96]{1,0:T(4,128)} %keep_ref.3, s32[1]{0:T(128)} %bitcast.13.base_ref, s32[3,128]{1,0:T(4,128)} %copy-done.1, bf16[8,384,128]{2,1,0:T(8,128)(2,1)} %bitcast.50, ...), custom_call_target="tpu_custom_call" | custom-call | flops 1610612736 | bytes 2457600 | tf_op jit(solution)/shard_map/pallas_call | solution.py:191
  106.0 17.4 %all_to_all.51 = bf16[8,48,1024]{2,1,0:T(8,128)(2,1)S(1)} all-to-all(bf16[8,48,1024]{2,1,0:T(8,128)(2,1)} %bitcast.51), channel_id=1, replica_groups=mesh['ctx'=32,'kvh'=8] {'kvh'}, dimensions={0} | all-to-all | bytes 1572864 | tf_op jit(solution)/shard_map/all_to_all | solution.py:322
  123.3 0.9 copy.45
  (70 shorter events, 14.5 us)
Async XLA Ops:
  0.0 4.9 %copy-start = (bf16[48,1024]{1,0:T(8,128)(2,1)S(1)}, bf16[48,1024]{1,0:T(8,128)(2,1)}, u32[]{:S(2)}) copy-start(bf16[48,1024]{1,0:T(8,128)(2,1)} %param.15) | copy-start | bytes 294916
  0.0 22.7 %copy-start.3 = (s32[3,96]{1,0:T(4,128)S(1)}, s32[3,96]{1,0:T(4,128)}, u32[]{:S(2)}) copy-start(s32[3,96]{1,0:T(4,128)} %keep_ref.3) | copy-start | bytes 3460
  0.8 14.6 %collective-permute-start.2 = (s32[8]{0:T(128)S(1)}, s32[8]{0:T(128)S(1)}, u32[]{:S(2)}, u32[]{:S(2)}) collective-permute-start(s32[8]{0:T(128)S(1)} %convert_reduce_fusion.2), channel_id=1, source_target_pairs={{0,24},{8,0},{16,8},{24,16},{32,56},{40,32},{48,40},{56,48},{64,88... | collective-permute-start | bytes 104 | tf_op jit(solution)/shard_map/ppermute | solution.py:218
  1.7 13.7 %collective-permute-start.1 = (s32[8]{0:T(128)S(1)}, s32[8]{0:T(128)S(1)}, u32[]{:S(2)}, u32[]{:S(2)}) collective-permute-start(s32[8]{0:T(128)S(1)} %convert_reduce_fusion.2), channel_id=1, source_target_pairs={{0,16},{8,24},{16,0},{24,8},{32,48},{40,56},{48,32},{56,40},{64,80... | collective-permute-start | bytes 104 | tf_op jit(solution)/shard_map/ppermute | solution.py:218
  2.8 12.6 %collective-permute-start = (s32[8]{0:T(128)S(1)}, s32[8]{0:T(128)S(1)}, u32[]{:S(2)}, u32[]{:S(2)}) collective-permute-start(s32[8]{0:T(128)S(1)} %convert_reduce_fusion.2), channel_id=1, source_target_pairs={{0,8},{8,16},{16,24},{24,0},{32,40},{40,48},{48,56},{56,32},{64,72... | collective-permute-start | bytes 104 | tf_op jit(solution)/shard_map/ppermute | solution.py:218
  6.6 11.3 %all-to-all-start = ((bf16[48,8,256]{2,0,1:T(8,128)(2,1)}), bf16[48,8,256]{2,0,1:T(8,128)(2,1)S(1)}, u32[]{:S(2)}, u32[]{:S(2)}) async-start(bf16[48,8,256]{2,0,1:T(8,128)(2,1)} %pad_maximum_fusion.3), calls=%async_computation | async-start | bytes 393216 | tf_op jit(solution)/shard_map/all_to_all | solution.py:227
  17.9 27.9 %all-to-all-start.1 = ((bf16[48,8,1024]{2,0,1:T(8,128)(2,1)}), bf16[48,8,1024]{2,0,1:T(8,128)(2,1)S(1)}, u32[]{:S(2)}, u32[]{:S(2)}) async-start(bf16[48,8,1024]{2,0,1:T(8,128)(2,1)} %bitcast.40), calls=%async_computation.1 | async-start | bytes 1572864 | tf_op jit(solution)/shard_map/all_to_all | solution.py:228
  21.5 7.5 %collective-permute-start.3 = (bf16[400,256]{1,0:T(8,128)(2,1)S(1)}, bf16[400,256]{1,0:T(8,128)(2,1)S(1)}, u32[]{:S(2)}, u32[]{:S(2)}) collective-permute-start(bf16[400,256]{1,0:T(8,128)(2,1)S(1)} %pad_maximum_fusion.2), channel_id=1, source_target_pairs={{0,32},{8,40},{16,48},{24,56},{32,64},{40,72},{48,80},{56,88},{64,... | collective-permute-start | bytes 614408 | tf_op jit(solution)/shard_map/ppermute | solution.py:218
  28.9 7.1 %collective-permute-start.4 = (bf16[400,256]{1,0:T(8,128)(2,1)S(1)}, bf16[400,256]{1,0:T(8,128)(2,1)S(1)}, u32[]{:S(2)}, u32[]{:S(2)}) collective-permute-start(bf16[400,256]{1,0:T(8,128)(2,1)S(1)} %collective-permute-done.3), channel_id=1, source_target_pairs={{0,32},{8,40},{16,48},{24,56},{32,64},{40,72},{48,80},{56,88},{64,... | collective-permute-start | bytes 614408 | tf_op jit(solution)/shard_map/ppermute | solution.py:218
  36.0 6.9 %collective-permute-start.5 = (bf16[400,256]{1,0:T(8,128)(2,1)S(1)}, bf16[400,256]{1,0:T(8,128)(2,1)S(1)}, u32[]{:S(2)}, u32[]{:S(2)}) collective-permute-start(bf16[400,256]{1,0:T(8,128)(2,1)S(1)} %collective-permute-done.4), channel_id=1, source_target_pairs={{0,32},{8,40},{16,48},{24,56},{32,64},{40,72},{48,80},{56,88},{64,... | collective-permute-start | bytes 614408 | tf_op jit(solution)/shard_map/ppermute | solution.py:218
  43.0 6.7 %collective-permute-start.6 = (bf16[400,256]{1,0:T(8,128)(2,1)S(1)}, bf16[400,256]{1,0:T(8,128)(2,1)S(1)}, u32[]{:S(2)}, u32[]{:S(2)}) collective-permute-start(bf16[400,256]{1,0:T(8,128)(2,1)S(1)} %collective-permute-done.5), channel_id=1, source_target_pairs={{0,32},{8,40},{16,48},{24,56},{32,64},{40,72},{48,80},{56,88},{64,... | collective-permute-start | bytes 614408 | tf_op jit(solution)/shard_map/ppermute | solution.py:218
  43.8 7.6 %copy-start.2 = (s32[384]{0:T(512)S(1)}, s32[384]{0:T(512)}, u32[]{:S(2)}) copy-start(s32[384]{0:T(512)} %param.17) | copy-start | bytes 4612
  43.8 14.8 %collective-permute-start.7 = (bf16[800,256]{1,0:T(8,128)(2,1)}, bf16[800,256]{1,0:T(8,128)(2,1)S(1)}, u32[]{:S(2)}, u32[]{:S(2)}) collective-permute-start(bf16[800,256]{1,0:T(8,128)(2,1)} %get-tuple-element.53), channel_id=1, source_target_pairs={{0,8},{8,16},{16,24},{24,0},{32,40},{40,48},{48,56},{56,32},{64,72... | collective-permute-start | bytes 1228808 | tf_op jit(solution)/shard_map/ppermute | solution.py:218
  44.7 16.2 %collective-permute-start.8 = (bf16[800,256]{1,0:T(8,128)(2,1)}, bf16[800,256]{1,0:T(8,128)(2,1)S(1)}, u32[]{:S(2)}, u32[]{:S(2)}) collective-permute-start(bf16[800,256]{1,0:T(8,128)(2,1)} %get-tuple-element.53), channel_id=1, source_target_pairs={{0,24},{8,0},{16,8},{24,16},{32,56},{40,32},{48,40},{56,48},{64,88... | collective-permute-start | bytes 1228808 | tf_op jit(solution)/shard_map/ppermute | solution.py:218
  51.5 10.2 %copy-start.1 = (s32[3,128]{1,0:T(4,128)}, s32[3,128]{1,0:T(4,128)S(1)}, u32[]{:S(2)}) copy-start(s32[3,128]{1,0:T(4,128)S(1)} %add_bitcast_fusion.qds_ref) | copy-start | bytes 4612
  54.3 22.1 %collective-permute-start.10 = (bf16[800,256]{1,0:T(8,128)(2,1)S(1)}, bf16[800,256]{1,0:T(8,128)(2,1)S(1)}, u32[]{:S(2)}, u32[]{:S(2)}) collective-permute-start(bf16[800,256]{1,0:T(8,128)(2,1)S(1)} %get-tuple-element.52), channel_id=1, source_target_pairs={{0,8},{8,16},{16,24},{24,0},{32,40},{40,48},{48,56},{56,32},{64,72... | collective-permute-start | bytes 1228808 | tf_op jit(solution)/shard_map/ppermute | solution.py:218
  55.3 18.7 %collective-permute-start.11 = (bf16[800,256]{1,0:T(8,128)(2,1)S(1)}, bf16[800,256]{1,0:T(8,128)(2,1)S(1)}, u32[]{:S(2)}, u32[]{:S(2)}) collective-permute-start(bf16[800,256]{1,0:T(8,128)(2,1)S(1)} %get-tuple-element.51), channel_id=1, source_target_pairs={{0,24},{8,0},{16,8},{24,16},{32,56},{40,32},{48,40},{56,48},{64,88... | collective-permute-start | bytes 1228808 | tf_op jit(solution)/shard_map/ppermute | solution.py:218
  56.4 25.3 %collective-permute-start.13 = (bf16[400,256]{1,0:T(8,128)(2,1)S(1)}, bf16[400,256]{1,0:T(8,128)(2,1)S(1)}, u32[]{:S(2)}, u32[]{:S(2)}) collective-permute-start(bf16[400,256]{1,0:T(8,128)(2,1)S(1)} %get-tuple-element.47), channel_id=1, source_target_pairs={{0,16},{8,24},{16,0},{24,8},{32,48},{40,56},{48,32},{56,40},{64,80... | collective-permute-start | bytes 614408 | tf_op jit(solution)/shard_map/ppermute | solution.py:218
  58.5 17.1 %collective-permute-start.9 = (bf16[800,256]{1,0:T(8,128)(2,1)S(1)}, bf16[800,256]{1,0:T(8,128)(2,1)S(1)}, u32[]{:S(2)}, u32[]{:S(2)}) collective-permute-start(bf16[800,256]{1,0:T(8,128)(2,1)S(1)} %collective-permute-done.7), channel_id=1, source_target_pairs={{0,8},{8,16},{16,24},{24,0},{32,40},{40,48},{48,56},{56,32},{64,72... | collective-permute-start | bytes 1228808 | tf_op jit(solution)/shard_map/ppermute | solution.py:218
  73.9 7.0 %collective-permute-start.12 = (bf16[400,256]{1,0:T(8,128)(2,1)S(1)}, bf16[400,256]{1,0:T(8,128)(2,1)S(1)}, u32[]{:S(2)}, u32[]{:S(2)}) collective-permute-start(bf16[400,256]{1,0:T(8,128)(2,1)S(1)} %slice.62), channel_id=1, source_target_pairs={{0,24},{8,0},{16,8},{24,16},{32,56},{40,32},{48,40},{56,48},{64,88... | collective-permute-start | bytes 614408 | tf_op jit(solution)/shard_map/ppermute | solution.py:218
where the time goes:
time: 124 us
  Pallas kernels  35.9 us (29%)
  waiting for transfers between devices  25.2 us (20%)
  starting transfers between devices  21.8 us (18%)
  blocking collectives  17.4 us (14%)
  local copies, waits for them, and re-layouts  16.4 us (13%)
  other arithmetic  7.44 us (6%)
    pallas_call x2, Pallas kernels, attend_call(): pl.pallas_call(kernel, grid_spec=grid_spec, out_shape=out_shape, cost_est...  35.9 us
    ppermute x14, waiting for transfers between devices, shift(): return lax.ppermute(x, 'ctx', pairs)  23.1 us
    all_to_all x1, blocking collectives, local(): lax.all_to_all(outputs, 'kvh', split_axis=0, concat_axis=1, tiled=True)  17.4 us
    ppermute x14, starting transfers between devices, shift(): return lax.ppermute(x, 'ctx', pairs)  13.8 us
    unnamed x20, local copies, waits for them, and re-layouts  7.66 us
    all_to_all x1, starting transfers between devices, local(): lax.all_to_all(kv, 'kvh', split_axis=1, concat_axis=0, tiled=True)  4.47 us
    all_to_all x1, starting transfers between devices, local(): lax.all_to_all(queries, 'kvh', split_axis=1, concat_axis=0, tiled=True)  3.55 us
  transfers between devices with their start and end apart: 16, of which 7 were waited for; matrix products, arithmetic and copies ran while one was open for 17% of the time, Pallas kernels for 10%

commit v1 on v0

--- a/solution.py
+++ b/solution.py
@@ -282,8 +282,8 @@
         relay = l_minus[: prow * len(late)]
         add(shift(relay, x_pairs(nx - 1)), [(a, 2) for a in late])
     add(shift(extra[2], x_pairs(2)), [("e", 2)])
-    kv_own = jnp.concatenate(parts[:reach + 1], axis=0)
-    kv_rest = jnp.concatenate(parts[reach + 1:], axis=0)
+    kv_own = jnp.concatenate(parts[:reach + 3], axis=0)
+    kv_rest = jnp.concatenate(parts[reach + 3:], axis=0)
 
     n_slots = len(tags)
     table = np.zeros((reach + 1, nx), np.int32)
@@ -293,7 +293,8 @@
             table[reach, d] = s
         else:
             table[a, d] = s
-    tails = kv_own.reshape(reach + 1, prow, -1)[:, rows_here:rows_here + 2, :nx * N_DOC_IDS]
+    tails = kv_own[: (reach + 1) * prow].reshape(reach + 1, prow, -1)
+    tails = tails[:, rows_here:rows_here + 2, :nx * N_DOC_IDS]
     tails = tails.astype(jnp.int32)
     below_col = (tails[:, 0, :] * 32 + tails[:, 1, :]).reshape(reach + 1, nx, N_DOC_IDS)
     a_ids = np.arange(reach + 1)[:, None]

time: 124 us -> 126 us (1.016)
  the two profiles are of different devices: /device:TPU:166 before, /device:TPU:132 now
where the time goes in v1:
time: 126 us
  Pallas kernels  34.7 us (28%)
  waiting for transfers between devices  27.5 us (22%)
  starting transfers between devices  22.9 us (18%)
  blocking collectives  17.4 us (14%)
  local copies, waits for them, and re-layouts  14.9 us (12%)
  other arithmetic  8.7 us (7%)
    pallas_call x2, Pallas kernels, attend_call(): pl.pallas_call(kernel, grid_spec=grid_spec, out_shape=out_shape, cost_est...  34.7 us
    ppermute x14, waiting for transfers between devices, shift(): return lax.ppermute(x, 'ctx', pairs)  25.8 us
    all_to_all x1, blocking collectives, local(): lax.all_to_all(outputs, 'kvh', split_axis=0, concat_axis=1, tiled=True)  17.4 us
    ppermute x14, starting transfers between devices, shift(): return lax.ppermute(x, 'ctx', pairs)  14.9 us
    unnamed x24, local copies, waits for them, and re-layouts  6.1 us
    all_to_all x1, starting transfers between devices, local(): lax.all_to_all(kv, 'kvh', split_axis=1, concat_axis=0, tiled=True)  4.47 us
    all_to_all x1, starting transfers between devices, local(): lax.all_to_all(queries, 'kvh', split_axis=1, concat_axis=0, tiled=True)  3.55 us
  transfers between devices with their start and end apart: 16, of which 6 were waited for; matrix products, arithmetic and copies ran while one was open for 16% of the time, Pallas kernels for 15%

profile of v1, /device:TPU:132, one launch (start us, length us, event | category | flops | bytes accessed | tf_op | source)
XLA Modules:
  0.0 126.3 jit_solution(13533735431944270395)
XLA Ops:
  0.0 0.8 convert_reduce_fusion.2
  0.8 1.3 %collective-permute-start = (s32[8]{0:T(128)S(1)}, s32[8]{0:T(128)S(1)}, u32[]{:S(2)}, u32[]{:S(2)}) collective-permute-start(s32[8]{0:T(128)S(1)} %convert_reduce_fusion.2), channel_id=1, source_target_pairs={{0,8},{8,16},{16,24},{24,0},{32,40},{40,48},{48,56},{56,32},{64,72... | collective-permute-start | bytes 104 | tf_op jit(solution)/shard_map/ppermute | solution.py:218
  2.1 0.8 collective-permute-start.1
  2.9 1.1 collective-permute-start.2
  4.0 0.9 copy_bitcast_fusion.2
  5.7 4.5 %all-to-all-start = ((bf16[48,8,256]{2,0,1:T(8,128)(2,1)}), bf16[48,8,256]{2,0,1:T(8,128)(2,1)S(1)}, u32[]{:S(2)}, u32[]{:S(2)}) async-start(bf16[48,8,256]{2,0,1:T(8,128)(2,1)} %pad_maximum_fusion.3), calls=%async_computation | async-start | bytes 393216 | tf_op jit(solution)/shard_map/all_to_all | solution.py:227
  12.9 2.1 %copy.52 = bf16[6,8,8,1024]{3,2,0,1:T(8,128)(2,1)} copy(bf16[6,8,8,1024]{3,2,1,0:T(8,128)(2,1)} %bitcast.48) | data formatting | bytes 1572864 | tf_op jit(solution)/shard_map/all_to_all | solution.py:228
  15.3 1.6 %all-to-all-done = bf16[48,8,256]{2,0,1:T(8,128)(2,1)S(1)} async-done(((bf16[48,8,256]{2,0,1:T(8,128)(2,1)}), bf16[48,8,256]{2,0,1:T(8,128)(2,1)S(1)}, u32[]{:S(2)}, u32[]{:S(2)}) %all-to-all-start) | async-done | bytes 196640 | tf_op jit(solution)/shard_map/all_to_all | solution.py:227
  17.0 3.5 %all-to-all-start.1 = ((bf16[48,8,1024]{2,0,1:T(8,128)(2,1)}), bf16[48,8,1024]{2,0,1:T(8,128)(2,1)S(1)}, u32[]{:S(2)}, u32[]{:S(2)}) async-start(bf16[48,8,1024]{2,0,1:T(8,128)(2,1)} %bitcast.40), calls=%async_computation.1 | async-start | bytes 1572864 | tf_op jit(solution)/shard_map/all_to_all | solution.py:228
  20.6 1.1 collective-permute-start.3
  22.0 7.3 %collective-permute-done.3 = bf16[400,256]{1,0:T(8,128)(2,1)S(1)} collective-permute-done((bf16[400,256]{1,0:T(8,128)(2,1)S(1)}, bf16[400,256]{1,0:T(8,128)(2,1)S(1)}, u32[]{:S(2)}, u32[]{:S(2)}) %collective-permute-start.3) | collective-permute-done | bytes 204832 | tf_op jit(solution)/shard_map/ppermute | solution.py:218
  30.0 7.1 %collective-permute-done.4 = bf16[400,256]{1,0:T(8,128)(2,1)S(1)} collective-permute-done((bf16[400,256]{1,0:T(8,128)(2,1)S(1)}, bf16[400,256]{1,0:T(8,128)(2,1)S(1)}, u32[]{:S(2)}, u32[]{:S(2)}) %collective-permute-start.4) | collective-permute-done | bytes 204832 | tf_op jit(solution)/shard_map/ppermute | solution.py:218
  37.7 0.8 constant_dynamic-update-slice_fusion.18
  38.5 5.5 %collective-permute-done.5 = bf16[400,256]{1,0:T(8,128)(2,1)S(1)} collective-permute-done((bf16[400,256]{1,0:T(8,128)(2,1)S(1)}, bf16[400,256]{1,0:T(8,128)(2,1)S(1)}, u32[]{:S(2)}, u32[]{:S(2)}) %collective-permute-start.5) | collective-permute-done | bytes 204832 | tf_op jit(solution)/shard_map/ppermute | solution.py:218
  44.1 0.8 constant_dynamic-update-slice_fusion.17
  44.9 1.0 collective-permute-start.7
  45.9 2.2 %collective-permute-start.13 = (bf16[800,256]{1,0:T(8,128)(2,1)}, bf16[800,256]{1,0:T(8,128)(2,1)S(1)}, u32[]{:S(2)}, u32[]{:S(2)}) collective-permute-start(bf16[800,256]{1,0:T(8,128)(2,1)} %get-tuple-element.54), channel_id=1, source_target_pairs={{0,24},{8,0},{16,8},{24,16},{32,56},{40,32},{48,40},{56,48},{64,88... | collective-permute-start | bytes 1228808 | tf_op jit(solution)/shard_map/ppermute | solution.py:218
  48.2 1.0 copy.53
  50.0 1.0 collective-permute-done.6
  51.0 0.9 broadcast_select_fusion
  52.9 1.0 collective-permute-start.9
  54.0 1.3 %collective-permute-start.10 = (bf16[800,256]{1,0:T(8,128)(2,1)S(1)}, bf16[800,256]{1,0:T(8,128)(2,1)S(1)}, u32[]{:S(2)}, u32[]{:S(2)}) collective-permute-start(bf16[800,256]{1,0:T(8,128)(2,1)S(1)} %get-tuple-element.60), channel_id=1, source_target_pairs={{0,24},{8,0},{16,8},{24,16},{32,56},{40,32},{48,40},{56,48},{64,88... | collective-permute-start | bytes 1228808 | tf_op jit(solution)/shard_map/ppermute | solution.py:218
  55.2 4.0 %collective-permute-start.12 = (bf16[400,256]{1,0:T(8,128)(2,1)S(1)}, bf16[400,256]{1,0:T(8,128)(2,1)S(1)}, u32[]{:S(2)}, u32[]{:S(2)}) collective-permute-start(bf16[400,256]{1,0:T(8,128)(2,1)S(1)} %get-tuple-element.47), channel_id=1, source_target_pairs={{0,16},{8,24},{16,0},{24,8},{32,48},{40,56},{48,32},{56,40},{64,80... | collective-permute-start | bytes 614408 | tf_op jit(solution)/shard_map/ppermute | solution.py:218
  62.2 1.7 %sort.23 = (s32[3,96]{0,1:T(8,128)}, s32[3,96]{0,1:T(8,128)}, s32[3,96]{0,1:T(8,128)}) sort(s32[3,96]{0,1:T(8,128)S(1)} %get-tuple-element.65, s32[3,96]{0,1:T(8,128)S(1)} %get-tuple-element.64, s32[3,96]{0,1:T(8,128)S(1)} %iota.44), dimensions={1}, to_apply=%region_5.6 | sort | flops 2592 | bytes 6912 | tf_op jit(solution)/shard_map/sort | solution.py:138
  64.0 1.4 %copy.39.tab_ref = s32[3,96]{1,0:T(4,128)} copy(s32[3,96]{0,1:T(8,128)} %get-tuple-element.35) | data formatting | bytes 2304 | tf_op jit(solution)/shard_map/sort | solution.py:138
  66.2 18.5 %shard_map.100 = (f32[384,1024]{1,0:T(8,128)}, f32[24,1024]{1,0:T(8,128)}, f32[24,1024]{1,0:T(8,128)}) custom-call(s32[3,96]{1,0:T(4,128)} %copy.39.tab_ref, s32[3,2]{1,0:T(4,128)} %get-tuple-element.68.cnt_ref, s32[3,96]{1,0:T(4,128)} %keep_ref.3, s32[1]{0:T(128)} %bitcast.13.base_ref, s32[3,128]{1,0:T(4,128)} %copy-done.3, bf16[8,384,128]{2,1,0:T(8,128)(2,1)} %bitcast.49, ...), custom_call_target="tpu_custom_call" | custom-call | flops 1610612736 | bytes 1843200 | tf_op jit(solution)/shard_map/pallas_call | solution.py:191
  84.8 0.9 collective-permute-start.11
  85.8 4.8 %collective-permute-done.11 = bf16[400,256]{1,0:T(8,128)(2,1)S(1)} collective-permute-done((bf16[400,256]{1,0:T(8,128)(2,1)S(1)}, bf16[400,256]{1,0:T(8,128)(2,1)S(1)}, u32[]{:S(2)}, u32[]{:S(2)}) %collective-permute-start.11) | collective-permute-done | bytes 204832 | tf_op jit(solution)/shard_map/ppermute | solution.py:218
  90.7 1.2 copy-done.1
  91.8 16.2 %shard_map.101 = bf16[384,1024]{1,0:T(8,128)(2,1)} custom-call(s32[3,96]{1,0:T(4,128)} %copy.39.tab_ref, s32[3,2]{1,0:T(4,128)} %get-tuple-element.69.cnt_ref, s32[3,96]{1,0:T(4,128)} %keep_ref.3, s32[1]{0:T(128)} %bitcast.13.base_ref, s32[3,128]{1,0:T(4,128)} %copy-done.3, bf16[8,384,128]{2,1,0:T(8,128)(2,1)} %bitcast.50, bf16[3200,256]{1,0:T(8,128)(2,1)} %copy-done.1, ...), custom_call_target="tpu_custom_call" | custom-call | flops 1610612736 | bytes 1638400 | tf_op jit(solution)/shard_map/pallas_call | solution.py:191
  108.0 17.4 %all_to_all.51 = bf16[8,48,1024]{2,1,0:T(8,128)(2,1)S(1)} all-to-all(bf16[8,48,1024]{2,1,0:T(8,128)(2,1)} %bitcast.51), channel_id=1, replica_groups=mesh['ctx'=32,'kvh'=8] {'kvh'}, dimensions={0} | all-to-all | bytes 1572864 | tf_op jit(solution)/shard_map/all_to_all | solution.py:323
  125.4 0.9 copy.45
  (74 shorter events, 11.3 us)
Async XLA Ops:
  0.0 4.0 %copy-start = (bf16[48,1024]{1,0:T(8,128)(2,1)S(1)}, bf16[48,1024]{1,0:T(8,128)(2,1)}, u32[]{:S(2)}) copy-start(bf16[48,1024]{1,0:T(8,128)(2,1)} %param.15) | copy-start | bytes 294916
  0.8 14.2 %collective-permute-start = (s32[8]{0:T(128)S(1)}, s32[8]{0:T(128)S(1)}, u32[]{:S(2)}, u32[]{:S(2)}) collective-permute-start(s32[8]{0:T(128)S(1)} %convert_reduce_fusion.2), channel_id=1, source_target_pairs={{0,8},{8,16},{16,24},{24,0},{32,40},{40,48},{48,56},{56,32},{64,72... | collective-permute-start | bytes 104 | tf_op jit(solution)/shard_map/ppermute | solution.py:218
  2.1 12.9 %collective-permute-start.1 = (s32[8]{0:T(128)S(1)}, s32[8]{0:T(128)S(1)}, u32[]{:S(2)}, u32[]{:S(2)}) collective-permute-start(s32[8]{0:T(128)S(1)} %convert_reduce_fusion.2), channel_id=1, source_target_pairs={{0,16},{8,24},{16,0},{24,8},{32,48},{40,56},{48,32},{56,40},{64,80... | collective-permute-start | bytes 104 | tf_op jit(solution)/shard_map/ppermute | solution.py:218
  2.9 12.1 %collective-permute-start.2 = (s32[8]{0:T(128)S(1)}, s32[8]{0:T(128)S(1)}, u32[]{:S(2)}, u32[]{:S(2)}) collective-permute-start(s32[8]{0:T(128)S(1)} %convert_reduce_fusion.2), channel_id=1, source_target_pairs={{0,24},{8,0},{16,8},{24,16},{32,56},{40,32},{48,40},{56,48},{64,88... | collective-permute-start | bytes 104 | tf_op jit(solution)/shard_map/ppermute | solution.py:218
  5.7 11.3 %all-to-all-start = ((bf16[48,8,256]{2,0,1:T(8,128)(2,1)}), bf16[48,8,256]{2,0,1:T(8,128)(2,1)S(1)}, u32[]{:S(2)}, u32[]{:S(2)}) async-start(bf16[48,8,256]{2,0,1:T(8,128)(2,1)} %pad_maximum_fusion.3), calls=%async_computation | async-start | bytes 393216 | tf_op jit(solution)/shard_map/all_to_all | solution.py:227
  10.1 11.7 %copy-start.5 = (s32[3,96]{1,0:T(4,128)S(1)}, s32[3,96]{1,0:T(4,128)}, u32[]{:S(2)}) copy-start(s32[3,96]{1,0:T(4,128)} %keep_ref.3) | copy-start | bytes 3460
  17.0 31.0 %all-to-all-start.1 = ((bf16[48,8,1024]{2,0,1:T(8,128)(2,1)}), bf16[48,8,1024]{2,0,1:T(8,128)(2,1)S(1)}, u32[]{:S(2)}, u32[]{:S(2)}) async-start(bf16[48,8,1024]{2,0,1:T(8,128)(2,1)} %bitcast.40), calls=%async_computation.1 | async-start | bytes 1572864 | tf_op jit(solution)/shard_map/all_to_all | solution.py:228
  20.6 8.7 %collective-permute-start.3 = (bf16[400,256]{1,0:T(8,128)(2,1)S(1)}, bf16[400,256]{1,0:T(8,128)(2,1)S(1)}, u32[]{:S(2)}, u32[]{:S(2)}) collective-permute-start(bf16[400,256]{1,0:T(8,128)(2,1)S(1)} %pad_maximum_fusion.2), channel_id=1, source_target_pairs={{0,32},{8,40},{16,48},{24,56},{32,64},{40,72},{48,80},{56,88},{64,... | collective-permute-start | bytes 614408 | tf_op jit(solution)/shard_map/ppermute | solution.py:218
  29.3 7.8 %collective-permute-start.4 = (bf16[400,256]{1,0:T(8,128)(2,1)S(1)}, bf16[400,256]{1,0:T(8,128)(2,1)S(1)}, u32[]{:S(2)}, u32[]{:S(2)}) collective-permute-start(bf16[400,256]{1,0:T(8,128)(2,1)S(1)} %collective-permute-done.3), channel_id=1, source_target_pairs={{0,32},{8,40},{16,48},{24,56},{32,64},{40,72},{48,80},{56,88},{64,... | collective-permute-start | bytes 614408 | tf_op jit(solution)/shard_map/ppermute | solution.py:218
  37.1 7.0 %collective-permute-start.5 = (bf16[400,256]{1,0:T(8,128)(2,1)S(1)}, bf16[400,256]{1,0:T(8,128)(2,1)S(1)}, u32[]{:S(2)}, u32[]{:S(2)}) collective-permute-start(bf16[400,256]{1,0:T(8,128)(2,1)S(1)} %collective-permute-done.4), channel_id=1, source_target_pairs={{0,32},{8,40},{16,48},{24,56},{32,64},{40,72},{48,80},{56,88},{64,... | collective-permute-start | bytes 614408 | tf_op jit(solution)/shard_map/ppermute | solution.py:218
  44.1 7.0 %collective-permute-start.6 = (bf16[400,256]{1,0:T(8,128)(2,1)S(1)}, bf16[400,256]{1,0:T(8,128)(2,1)S(1)}, u32[]{:S(2)}, u32[]{:S(2)}) collective-permute-start(bf16[400,256]{1,0:T(8,128)(2,1)S(1)} %collective-permute-done.5), channel_id=1, source_target_pairs={{0,32},{8,40},{16,48},{24,56},{32,64},{40,72},{48,80},{56,88},{64,... | collective-permute-start | bytes 614408 | tf_op jit(solution)/shard_map/ppermute | solution.py:218
  44.9 1.0 copy-start.2
  44.9 14.7 %collective-permute-start.7 = (bf16[800,256]{1,0:T(8,128)(2,1)}, bf16[800,256]{1,0:T(8,128)(2,1)S(1)}, u32[]{:S(2)}, u32[]{:S(2)}) collective-permute-start(bf16[800,256]{1,0:T(8,128)(2,1)} %get-tuple-element.54), channel_id=1, source_target_pairs={{0,8},{8,16},{16,24},{24,0},{32,40},{40,48},{48,56},{56,32},{64,72... | collective-permute-start | bytes 1228808 | tf_op jit(solution)/shard_map/ppermute | solution.py:218
  45.9 19.5 %collective-permute-start.13 = (bf16[800,256]{1,0:T(8,128)(2,1)}, bf16[800,256]{1,0:T(8,128)(2,1)S(1)}, u32[]{:S(2)}, u32[]{:S(2)}) collective-permute-start(bf16[800,256]{1,0:T(8,128)(2,1)} %get-tuple-element.54), channel_id=1, source_target_pairs={{0,24},{8,0},{16,8},{24,16},{32,56},{40,32},{48,40},{56,48},{64,88... | collective-permute-start | bytes 1228808 | tf_op jit(solution)/shard_map/ppermute | solution.py:218
  48.2 4.6 %copy-start.4 = (s32[384]{0:T(512)S(1)}, s32[384]{0:T(512)}, u32[]{:S(2)}) copy-start(s32[384]{0:T(512)} %param.17) | copy-start | bytes 4612
  52.9 32.8 %collective-permute-start.9 = (bf16[800,256]{1,0:T(8,128)(2,1)S(1)}, bf16[800,256]{1,0:T(8,128)(2,1)S(1)}, u32[]{:S(2)}, u32[]{:S(2)}) collective-permute-start(bf16[800,256]{1,0:T(8,128)(2,1)S(1)} %get-tuple-element.61), channel_id=1, source_target_pairs={{0,8},{8,16},{16,24},{24,0},{32,40},{40,48},{48,56},{56,32},{64,72... | collective-permute-start | bytes 1228808 | tf_op jit(solution)/shard_map/ppermute | solution.py:218
  54.0 30.8 %collective-permute-start.10 = (bf16[800,256]{1,0:T(8,128)(2,1)S(1)}, bf16[800,256]{1,0:T(8,128)(2,1)S(1)}, u32[]{:S(2)}, u32[]{:S(2)}) collective-permute-start(bf16[800,256]{1,0:T(8,128)(2,1)S(1)} %get-tuple-element.60), channel_id=1, source_target_pairs={{0,24},{8,0},{16,8},{24,16},{32,56},{40,32},{48,40},{56,48},{64,88... | collective-permute-start | bytes 1228808 | tf_op jit(solution)/shard_map/ppermute | solution.py:218
  55.2 35.4 %collective-permute-start.12 = (bf16[400,256]{1,0:T(8,128)(2,1)S(1)}, bf16[400,256]{1,0:T(8,128)(2,1)S(1)}, u32[]{:S(2)}, u32[]{:S(2)}) collective-permute-start(bf16[400,256]{1,0:T(8,128)(2,1)S(1)} %get-tuple-element.47), channel_id=1, source_target_pairs={{0,16},{8,24},{16,0},{24,8},{32,48},{40,56},{48,32},{56,40},{64,80... | collective-permute-start | bytes 614408 | tf_op jit(solution)/shard_map/ppermute | solution.py:218
  59.3 6.9 %copy-start.3 = (s32[3,128]{1,0:T(4,128)}, s32[3,128]{1,0:T(4,128)S(1)}, u32[]{:S(2)}) copy-start(s32[3,128]{1,0:T(4,128)S(1)} %add_bitcast_fusion.qds_ref) | copy-start | bytes 4612
  59.6 26.1 %collective-permute-start.8 = (bf16[800,256]{1,0:T(8,128)(2,1)S(1)}, bf16[800,256]{1,0:T(8,128)(2,1)S(1)}, u32[]{:S(2)}, u32[]{:S(2)}) collective-permute-start(bf16[800,256]{1,0:T(8,128)(2,1)S(1)} %collective-permute-done.7), channel_id=1, source_target_pairs={{0,8},{8,16},{16,24},{24,0},{32,40},{40,48},{48,56},{56,32},{64,72... | collective-permute-start | bytes 1228808 | tf_op jit(solution)/shard_map/ppermute | solution.py:218
  84.8 5.8 %collective-permute-start.11 = (bf16[400,256]{1,0:T(8,128)(2,1)S(1)}, bf16[400,256]{1,0:T(8,128)(2,1)S(1)}, u32[]{:S(2)}, u32[]{:S(2)}) collective-permute-start(bf16[400,256]{1,0:T(8,128)(2,1)S(1)} %slice.64), channel_id=1, source_target_pairs={{0,24},{8,0},{16,8},{24,16},{32,56},{40,32},{48,40},{56,48},{64,88... | collective-permute-start | bytes 614408 | tf_op jit(solution)/shard_map/ppermute | solution.py:218
  90.7 1.2 copy-start.1

commit v2 on v1

--- a/solution.py
+++ b/solution.py
@@ -279,8 +279,7 @@
     add(l_plus, [(a, 1) for a in late] + [("e", 1)])
     add(l_minus, [(a, nx - 1) for a in late] + [("e", nx - 1)])
     if late:
-        relay = l_minus[: prow * len(late)]
-        add(shift(relay, x_pairs(nx - 1)), [(a, 2) for a in late])
+        add(shift(blocks(late), x_pairs(2)), [(a, 2) for a in late])
     add(shift(extra[2], x_pairs(2)), [("e", 2)])
     kv_own = jnp.concatenate(parts[:reach + 3], axis=0)
     kv_rest = jnp.concatenate(parts[reach + 3:], axis=0)

time: 126 us -> 131 us (1.040)
  the two profiles are of different devices: /device:TPU:132 before, /device:TPU:162 now
where the time goes in v2:
time: 131 us; the launch traced here: 128 us
  Pallas kernels  33.2 us (25%)
  starting transfers between devices  29.1 us (22%)
  waiting for transfers between devices  20.9 us (16%)
  local copies, waits for them, and re-layouts  19.4 us (15%)
  blocking collectives  16.9 us (13%)
  other arithmetic  8.76 us (7%)
    pallas_call x2, Pallas kernels, attend_call(): pl.pallas_call(kernel, grid_spec=grid_spec, out_shape=out_shape, cost_est...  33.2 us
    ppermute x14, starting transfers between devices, shift(): return lax.ppermute(x, 'ctx', pairs)  21.1 us
    ppermute x14, waiting for transfers between devices, shift(): return lax.ppermute(x, 'ctx', pairs)  19.4 us
    all_to_all x1, blocking collectives, local(): lax.all_to_all(outputs, 'kvh', split_axis=0, concat_axis=1, tiled=True)  16.9 us
    unnamed x22, local copies, waits for them, and re-layouts  9.78 us
    all_to_all x1, starting transfers between devices, local(): lax.all_to_all(kv, 'kvh', split_axis=1, concat_axis=0, tiled=True)  4.47 us
    all_to_all x1, starting transfers between devices, local(): lax.all_to_all(queries, 'kvh', split_axis=1, concat_axis=0, tiled=True)  3.55 us
  transfers between devices with their start and end apart: 16, of which 7 were waited for; matrix products, arithmetic and copies ran while one was open for 18% of the time, Pallas kernels for 14%

profile of v2, /device:TPU:162, one launch (start us, length us, event | category | flops | bytes accessed | tf_op | source)
XLA Modules:
  0.0 128.5 jit_solution(8871118326854275297)
XLA Ops:
  0.0 0.8 convert_reduce_fusion.2
  0.8 1.6 %collective-permute-start = (s32[8]{0:T(128)S(1)}, s32[8]{0:T(128)S(1)}, u32[]{:S(2)}, u32[]{:S(2)}) collective-permute-start(s32[8]{0:T(128)S(1)} %convert_reduce_fusion.2), channel_id=1, source_target_pairs={{0,8},{8,16},{16,24},{24,0},{32,40},{40,48},{48,56},{56,32},{64,72... | collective-permute-start | bytes 104 | tf_op jit(solution)/shard_map/ppermute | solution.py:218
  2.4 1.1 collective-permute-start.1
  3.5 2.2 %collective-permute-start.2 = (s32[8]{0:T(128)S(1)}, s32[8]{0:T(128)S(1)}, u32[]{:S(2)}, u32[]{:S(2)}) collective-permute-start(s32[8]{0:T(128)S(1)} %convert_reduce_fusion.2), channel_id=1, source_target_pairs={{0,24},{8,0},{16,8},{24,16},{32,56},{40,32},{48,40},{56,48},{64,88... | collective-permute-start | bytes 104 | tf_op jit(solution)/shard_map/ppermute | solution.py:218
  5.7 0.9 copy_bitcast_fusion.2
  7.3 4.5 %all-to-all-start = ((bf16[48,8,256]{2,0,1:T(8,128)(2,1)}), bf16[48,8,256]{2,0,1:T(8,128)(2,1)S(1)}, u32[]{:S(2)}, u32[]{:S(2)}) async-start(bf16[48,8,256]{2,0,1:T(8,128)(2,1)} %pad_maximum_fusion.3), calls=%async_computation | async-start | bytes 393216 | tf_op jit(solution)/shard_map/all_to_all | solution.py:227
  14.5 2.1 %copy.52 = bf16[6,8,8,1024]{3,2,0,1:T(8,128)(2,1)} copy(bf16[6,8,8,1024]{3,2,1,0:T(8,128)(2,1)} %bitcast.48) | data formatting | bytes 1572864 | tf_op jit(solution)/shard_map/all_to_all | solution.py:228
  17.0 1.6 %all-to-all-done = bf16[48,8,256]{2,0,1:T(8,128)(2,1)S(1)} async-done(((bf16[48,8,256]{2,0,1:T(8,128)(2,1)}), bf16[48,8,256]{2,0,1:T(8,128)(2,1)S(1)}, u32[]{:S(2)}, u32[]{:S(2)}) %all-to-all-start) | async-done | bytes 196640 | tf_op jit(solution)/shard_map/all_to_all | solution.py:227
  18.6 3.5 %all-to-all-start.1 = ((bf16[48,8,1024]{2,0,1:T(8,128)(2,1)}), bf16[48,8,1024]{2,0,1:T(8,128)(2,1)S(1)}, u32[]{:S(2)}, u32[]{:S(2)}) async-start(bf16[48,8,1024]{2,0,1:T(8,128)(2,1)} %bitcast.40), calls=%async_computation.1 | async-start | bytes 1572864 | tf_op jit(solution)/shard_map/all_to_all | solution.py:228
  22.2 1.1 collective-permute-start.3
  23.6 6.1 %collective-permute-done.3 = bf16[400,256]{1,0:T(8,128)(2,1)S(1)} collective-permute-done((bf16[400,256]{1,0:T(8,128)(2,1)S(1)}, bf16[400,256]{1,0:T(8,128)(2,1)S(1)}, u32[]{:S(2)}, u32[]{:S(2)}) %collective-permute-start.3) | collective-permute-done | bytes 204832 | tf_op jit(solution)/shard_map/ppermute | solution.py:218
  29.7 1.0 collective-permute-start.4
  31.4 5.4 %collective-permute-done.4 = bf16[400,256]{1,0:T(8,128)(2,1)S(1)} collective-permute-done((bf16[400,256]{1,0:T(8,128)(2,1)S(1)}, bf16[400,256]{1,0:T(8,128)(2,1)S(1)}, u32[]{:S(2)}, u32[]{:S(2)}) %collective-permute-start.4) | collective-permute-done | bytes 204832 | tf_op jit(solution)/shard_map/ppermute | solution.py:218
  37.9 0.9 constant_dynamic-update-slice_fusion.18
  38.7 4.9 %collective-permute-done.5 = bf16[400,256]{1,0:T(8,128)(2,1)S(1)} collective-permute-done((bf16[400,256]{1,0:T(8,128)(2,1)S(1)}, bf16[400,256]{1,0:T(8,128)(2,1)S(1)}, u32[]{:S(2)}, u32[]{:S(2)}) %collective-permute-start.5) | collective-permute-done | bytes 204832 | tf_op jit(solution)/shard_map/ppermute | solution.py:218
  43.7 0.8 constant_dynamic-update-slice_fusion.17
  44.5 1.0 copy-done.1
  45.5 1.4 %collective-permute-start.13 = (bf16[800,256]{1,0:T(8,128)(2,1)}, bf16[800,256]{1,0:T(8,128)(2,1)S(1)}, u32[]{:S(2)}, u32[]{:S(2)}) collective-permute-start(bf16[800,256]{1,0:T(8,128)(2,1)} %get-tuple-element.54), channel_id=1, source_target_pairs={{0,24},{8,0},{16,8},{24,16},{32,56},{40,32},{48,40},{56,48},{64,88... | collective-permute-start | bytes 1228808 | tf_op jit(solution)/shard_map/ppermute | solution.py:218
  47.1 1.0 copy.53
  48.1 1.1 collective-permute-start.11
  50.4 0.9 broadcast_select_fusion
  52.3 2.3 %collective-permute-start.9 = (bf16[800,256]{1,0:T(8,128)(2,1)S(1)}, bf16[800,256]{1,0:T(8,128)(2,1)S(1)}, u32[]{:S(2)}, u32[]{:S(2)}) collective-permute-start(bf16[800,256]{1,0:T(8,128)(2,1)S(1)} %get-tuple-element.61), channel_id=1, source_target_pairs={{0,8},{8,16},{16,24},{24,0},{32,40},{40,48},{48,56},{56,32},{64,72... | collective-permute-start | bytes 1228808 | tf_op jit(solution)/shard_map/ppermute | solution.py:218
  54.9 2.2 %collective-permute-done.7 = bf16[800,256]{1,0:T(8,128)(2,1)S(1)} collective-permute-done((bf16[800,256]{1,0:T(8,128)(2,1)}, bf16[800,256]{1,0:T(8,128)(2,1)S(1)}, u32[]{:S(2)}, u32[]{:S(2)}) %collective-permute-start.7) | collective-permute-done | bytes 409632 | tf_op jit(solution)/shard_map/ppermute | solution.py:218
  58.3 0.8 constant_dynamic-update-slice_fusion.14
  59.3 8.5 %collective-permute-start.12 = (bf16[400,256]{1,0:T(8,128)(2,1)S(1)}, bf16[400,256]{1,0:T(8,128)(2,1)}, u32[]{:S(2)}, u32[]{:S(2)}) collective-permute-start(bf16[400,256]{1,0:T(8,128)(2,1)S(1)} %get-tuple-element.47), channel_id=1, source_target_pairs={{0,16},{8,24},{16,0},{24,8},{32,48},{40,56},{48,32},{56,40},{64,80... | collective-permute-start | bytes 614408 | tf_op jit(solution)/shard_map/ppermute | solution.py:218
  69.5 1.7 %sort.23 = (s32[3,96]{0,1:T(8,128)}, s32[3,96]{0,1:T(8,128)S(1)}, s32[3,96]{0,1:T(8,128)}) sort(s32[3,96]{0,1:T(8,128)S(1)} %get-tuple-element.65, s32[3,96]{0,1:T(8,128)S(1)} %get-tuple-element.64, s32[3,96]{0,1:T(8,128)S(1)} %iota.44), dimensions={1}, to_apply=%region_5.6 | sort | flops 2592 | bytes 6912 | tf_op jit(solution)/shard_map/sort | solution.py:138
  71.8 17.4 %shard_map.100 = (f32[384,1024]{1,0:T(8,128)}, f32[24,1024]{1,0:T(8,128)}, f32[24,1024]{1,0:T(8,128)}) custom-call(s32[3,96]{1,0:T(4,128)} %copy.39.tab_ref, s32[3,2]{1,0:T(4,128)} %get-tuple-element.68.cnt_ref, s32[3,96]{1,0:T(4,128)} %keep_ref.3, s32[1]{0:T(128)} %bitcast.13.base_ref, s32[3,128]{1,0:T(4,128)} %copy-done.2, bf16[8,384,128]{2,1,0:T(8,128)(2,1)} %bitcast.49, ...), custom_call_target="tpu_custom_call" | custom-call | flops 1610612736 | bytes 1843200 | tf_op jit(solution)/shard_map/pallas_call | solution.py:191
  91.5 1.6 %constant_dynamic-update-slice_fusion.9 = bf16[3200,256]{1,0:T(8,128)(2,1)} fusion(bf16[3200,256]{1,0:T(8,128)(2,1)} %constant_dynamic-update-slice_fusion.10, bf16[400,256]{1,0:T(8,128)(2,1)} %collective-permute-done.11), kind=kLoop, calls=%fused_computation.37 | loop fusion | bytes 409600
  93.2 1.6 %constant_dynamic-update-slice_fusion.8.kv_ref = bf16[3200,256]{1,0:T(8,128)(2,1)} fusion(bf16[3200,256]{1,0:T(8,128)(2,1)} %constant_dynamic-update-slice_fusion.9, bf16[400,256]{1,0:T(8,128)(2,1)} %collective-permute-done.12), kind=kLoop, calls=%fused_computation.36 | loop fusion | bytes 409600 | tf_op jit(solution)/shard_map/concatenate | solution.py:285
  94.8 15.9 %shard_map.101 = bf16[384,1024]{1,0:T(8,128)(2,1)} custom-call(s32[3,96]{1,0:T(4,128)} %copy.39.tab_ref, s32[3,2]{1,0:T(4,128)} %get-tuple-element.69.cnt_ref, s32[3,96]{1,0:T(4,128)} %keep_ref.3, s32[1]{0:T(128)} %bitcast.13.base_ref, s32[3,128]{1,0:T(4,128)} %copy-done.2, bf16[8,384,128]{2,1,0:T(8,128)(2,1)} %bitcast.50, ...), custom_call_target="tpu_custom_call" | custom-call | flops 1610612736 | bytes 1638400 | tf_op jit(solution)/shard_map/pallas_call | solution.py:191
  110.6 16.9 %all_to_all.51 = bf16[8,48,1024]{2,1,0:T(8,128)(2,1)S(1)} all-to-all(bf16[8,48,1024]{2,1,0:T(8,128)(2,1)} %bitcast.51), channel_id=1, replica_groups=mesh['ctx'=32,'kvh'=8] {'kvh'}, dimensions={0} | all-to-all | bytes 1572864 | tf_op jit(solution)/shard_map/all_to_all | solution.py:322
  127.5 0.9 copy.45
  (71 shorter events, 14.7 us)
Async XLA Ops:
  0.0 5.7 %copy-start = (bf16[48,1024]{1,0:T(8,128)(2,1)S(1)}, bf16[48,1024]{1,0:T(8,128)(2,1)}, u32[]{:S(2)}) copy-start(bf16[48,1024]{1,0:T(8,128)(2,1)} %param.15) | copy-start | bytes 294916
  0.8 15.8 %collective-permute-start = (s32[8]{0:T(128)S(1)}, s32[8]{0:T(128)S(1)}, u32[]{:S(2)}, u32[]{:S(2)}) collective-permute-start(s32[8]{0:T(128)S(1)} %convert_reduce_fusion.2), channel_id=1, source_target_pairs={{0,8},{8,16},{16,24},{24,0},{32,40},{40,48},{48,56},{56,32},{64,72... | collective-permute-start | bytes 104 | tf_op jit(solution)/shard_map/ppermute | solution.py:218
  2.4 14.3 %collective-permute-start.1 = (s32[8]{0:T(128)S(1)}, s32[8]{0:T(128)S(1)}, u32[]{:S(2)}, u32[]{:S(2)}) collective-permute-start(s32[8]{0:T(128)S(1)} %convert_reduce_fusion.2), channel_id=1, source_target_pairs={{0,16},{8,24},{16,0},{24,8},{32,48},{40,56},{48,32},{56,40},{64,80... | collective-permute-start | bytes 104 | tf_op jit(solution)/shard_map/ppermute | solution.py:218
  3.5 13.2 %collective-permute-start.2 = (s32[8]{0:T(128)S(1)}, s32[8]{0:T(128)S(1)}, u32[]{:S(2)}, u32[]{:S(2)}) collective-permute-start(s32[8]{0:T(128)S(1)} %convert_reduce_fusion.2), channel_id=1, source_target_pairs={{0,24},{8,0},{16,8},{24,16},{32,56},{40,32},{48,40},{56,48},{64,88... | collective-permute-start | bytes 104 | tf_op jit(solution)/shard_map/ppermute | solution.py:218
  7.3 11.3 %all-to-all-start = ((bf16[48,8,256]{2,0,1:T(8,128)(2,1)}), bf16[48,8,256]{2,0,1:T(8,128)(2,1)S(1)}, u32[]{:S(2)}, u32[]{:S(2)}) async-start(bf16[48,8,256]{2,0,1:T(8,128)(2,1)} %pad_maximum_fusion.3), calls=%async_computation | async-start | bytes 393216 | tf_op jit(solution)/shard_map/all_to_all | solution.py:227
  11.8 11.7 %copy-start.4 = (s32[3,96]{1,0:T(4,128)S(1)}, s32[3,96]{1,0:T(4,128)}, u32[]{:S(2)}) copy-start(s32[3,96]{1,0:T(4,128)} %keep_ref.3) | copy-start | bytes 3460
  18.6 28.3 %all-to-all-start.1 = ((bf16[48,8,1024]{2,0,1:T(8,128)(2,1)}), bf16[48,8,1024]{2,0,1:T(8,128)(2,1)S(1)}, u32[]{:S(2)}, u32[]{:S(2)}) async-start(bf16[48,8,1024]{2,0,1:T(8,128)(2,1)} %bitcast.40), calls=%async_computation.1 | async-start | bytes 1572864 | tf_op jit(solution)/shard_map/all_to_all | solution.py:228
  22.2 7.5 %collective-permute-start.3 = (bf16[400,256]{1,0:T(8,128)(2,1)S(1)}, bf16[400,256]{1,0:T(8,128)(2,1)S(1)}, u32[]{:S(2)}, u32[]{:S(2)}) collective-permute-start(bf16[400,256]{1,0:T(8,128)(2,1)S(1)} %pad_maximum_fusion.2), channel_id=1, source_target_pairs={{0,32},{8,40},{16,48},{24,56},{32,64},{40,72},{48,80},{56,88},{64,... | collective-permute-start | bytes 614408 | tf_op jit(solution)/shard_map/ppermute | solution.py:218
  29.7 7.1 %collective-permute-start.4 = (bf16[400,256]{1,0:T(8,128)(2,1)S(1)}, bf16[400,256]{1,0:T(8,128)(2,1)S(1)}, u32[]{:S(2)}, u32[]{:S(2)}) collective-permute-start(bf16[400,256]{1,0:T(8,128)(2,1)S(1)} %collective-permute-done.3), channel_id=1, source_target_pairs={{0,32},{8,40},{16,48},{24,56},{32,64},{40,72},{48,80},{56,88},{64,... | collective-permute-start | bytes 614408 | tf_op jit(solution)/shard_map/ppermute | solution.py:218
  36.8 6.9 %collective-permute-start.5 = (bf16[400,256]{1,0:T(8,128)(2,1)S(1)}, bf16[400,256]{1,0:T(8,128)(2,1)S(1)}, u32[]{:S(2)}, u32[]{:S(2)}) collective-permute-start(bf16[400,256]{1,0:T(8,128)(2,1)S(1)} %collective-permute-done.4), channel_id=1, source_target_pairs={{0,32},{8,40},{16,48},{24,56},{32,64},{40,72},{48,80},{56,88},{64,... | collective-permute-start | bytes 614408 | tf_op jit(solution)/shard_map/ppermute | solution.py:218
  43.7 6.7 %collective-permute-start.6 = (bf16[400,256]{1,0:T(8,128)(2,1)S(1)}, bf16[400,256]{1,0:T(8,128)(2,1)S(1)}, u32[]{:S(2)}, u32[]{:S(2)}) collective-permute-start(bf16[400,256]{1,0:T(8,128)(2,1)S(1)} %collective-permute-done.5), channel_id=1, source_target_pairs={{0,32},{8,40},{16,48},{24,56},{32,64},{40,72},{48,80},{56,88},{64,... | collective-permute-start | bytes 614408 | tf_op jit(solution)/shard_map/ppermute | solution.py:218
  44.5 1.0 copy-start.1
  44.5 12.6 %collective-permute-start.7 = (bf16[800,256]{1,0:T(8,128)(2,1)}, bf16[800,256]{1,0:T(8,128)(2,1)S(1)}, u32[]{:S(2)}, u32[]{:S(2)}) collective-permute-start(bf16[800,256]{1,0:T(8,128)(2,1)} %get-tuple-element.54), channel_id=1, source_target_pairs={{0,8},{8,16},{16,24},{24,0},{32,40},{40,48},{48,56},{56,32},{64,72... | collective-permute-start | bytes 1228808 | tf_op jit(solution)/shard_map/ppermute | solution.py:218
  45.5 13.9 %collective-permute-start.13 = (bf16[800,256]{1,0:T(8,128)(2,1)}, bf16[800,256]{1,0:T(8,128)(2,1)S(1)}, u32[]{:S(2)}, u32[]{:S(2)}) collective-permute-start(bf16[800,256]{1,0:T(8,128)(2,1)} %get-tuple-element.54), channel_id=1, source_target_pairs={{0,24},{8,0},{16,8},{24,16},{32,56},{40,32},{48,40},{56,48},{64,88... | collective-permute-start | bytes 1228808 | tf_op jit(solution)/shard_map/ppermute | solution.py:218
  47.1 5.1 %copy-start.3 = (s32[384]{0:T(512)S(1)}, s32[384]{0:T(512)}, u32[]{:S(2)}) copy-start(s32[384]{0:T(512)} %param.17) | copy-start | bytes 4612
  48.1 43.4 %collective-permute-start.11 = (bf16[400,256]{1,0:T(8,128)(2,1)S(1)}, bf16[400,256]{1,0:T(8,128)(2,1)}, u32[]{:S(2)}, u32[]{:S(2)}) collective-permute-start(bf16[400,256]{1,0:T(8,128)(2,1)S(1)} %collective-permute-done.5), channel_id=1, source_target_pairs={{0,16},{8,24},{16,0},{24,8},{32,48},{40,56},{48,32},{56,40},{64,80... | collective-permute-start | bytes 614408 | tf_op jit(solution)/shard_map/ppermute | solution.py:218
  52.3 37.6 %collective-permute-start.9 = (bf16[800,256]{1,0:T(8,128)(2,1)S(1)}, bf16[800,256]{1,0:T(8,128)(2,1)S(1)}, u32[]{:S(2)}, u32[]{:S(2)}) collective-permute-start(bf16[800,256]{1,0:T(8,128)(2,1)S(1)} %get-tuple-element.61), channel_id=1, source_target_pairs={{0,8},{8,16},{16,24},{24,0},{32,40},{40,48},{48,56},{56,32},{64,72... | collective-permute-start | bytes 1228808 | tf_op jit(solution)/shard_map/ppermute | solution.py:218
  54.6 36.1 %collective-permute-start.10 = (bf16[800,256]{1,0:T(8,128)(2,1)S(1)}, bf16[800,256]{1,0:T(8,128)(2,1)S(1)}, u32[]{:S(2)}, u32[]{:S(2)}) collective-permute-start(bf16[800,256]{1,0:T(8,128)(2,1)S(1)} %get-tuple-element.60), channel_id=1, source_target_pairs={{0,24},{8,0},{16,8},{24,16},{32,56},{40,32},{48,40},{56,48},{64,88... | collective-permute-start | bytes 1228808 | tf_op jit(solution)/shard_map/ppermute | solution.py:218
  54.6 17.2 %copy-start.2 = (s32[3,128]{1,0:T(4,128)}, s32[3,128]{1,0:T(4,128)S(1)}, u32[]{:S(2)}) copy-start(s32[3,128]{1,0:T(4,128)S(1)} %add_bitcast_fusion.qds_ref) | copy-start | bytes 4612
  57.1 32.0 %collective-permute-start.8 = (bf16[800,256]{1,0:T(8,128)(2,1)S(1)}, bf16[800,256]{1,0:T(8,128)(2,1)S(1)}, u32[]{:S(2)}, u32[]{:S(2)}) collective-permute-start(bf16[800,256]{1,0:T(8,128)(2,1)S(1)} %collective-permute-done.7), channel_id=1, source_target_pairs={{0,8},{8,16},{16,24},{24,0},{32,40},{40,48},{48,56},{56,32},{64,72... | collective-permute-start | bytes 1228808 | tf_op jit(solution)/shard_map/ppermute | solution.py:218
  59.3 33.8 %collective-permute-start.12 = (bf16[400,256]{1,0:T(8,128)(2,1)S(1)}, bf16[400,256]{1,0:T(8,128)(2,1)}, u32[]{:S(2)}, u32[]{:S(2)}) collective-permute-start(bf16[400,256]{1,0:T(8,128)(2,1)S(1)} %get-tuple-element.47), channel_id=1, source_target_pairs={{0,16},{8,24},{16,0},{24,8},{32,48},{40,56},{48,32},{56,40},{64,80... | collective-permute-start | bytes 614408 | tf_op jit(solution)/shard_map/ppermute | solution.py:218
